TPU v7x, 256 devices: a whole 4x4x8 slice. The times are simulated.
256 devices in a mesh: pos: 64 (over x, y_hi, z), section: 4 (over y_lo, core).
Axes of the slice: x: 4, y: 4 (y_hi: 2, y_lo: 2; y = y_hi * 2 + y_lo), z: 8, core: 2. Of those that a mesh axis runs over, the one named last changes fastest.
Arguments:
- sequence_features: bfloat16 [262144, 128], P('pos'), may hold values from -6 to 6
- norm_gain: float32 [4, 2, 128], P('section'), may hold values from 0.5 to 2
- conv_weight: bfloat16 [4, 2, 3, 128, 128], P('section'), may hold values from -0.3125 to 0.3125
- conv_bias: float32 [4, 2, 128], P('section'), may hold values from -3 to 3
- mix_weight: bfloat16 [4, 2, 128, 128], P('section'), may hold values from -0.5 to 0.5
Outputs:
- section_outputs: bfloat16 [4, 262144, 128], P('section', 'pos')
All inputs are finite; a program needn't handle non-finite values.
Results may differ from a plain program's by a relative error of at most 0.024.
Values may be sent and summed in bfloat16 or wider, within the bound.
No kernel may reach another device: no remote copies, remote signals or barrier semaphores. Data moves between devices by JAX's collectives and lax.ppermute only.
A program may use at most 64 MiB of HBM per device.

v0:
```python
import jax
import jax.numpy as jnp
from jax import lax
from jax.sharding import PartitionSpec as P

REDUNDANT = 5


def shifted(block, shift):
    count = lax.axis_size("pos")
    return lax.ppermute(block, "pos", [(i, (i + shift) % count) for i in range(count)])


def prepare(x, gain):
    r = x.astype(jnp.float32)
    meansq = jnp.mean(r * r, axis=-1, keepdims=True)
    return jax.nn.gelu(r * lax.rsqrt(meansq + 1e-06) * gain, approximate=False).astype(jnp.bfloat16)


def mix(x, before, h, after, taps, bias, mixing):
    conv = jnp.dot(h, taps[1], preferred_element_type=jnp.float32)
    conv = conv + jnp.dot(before, taps[0], preferred_element_type=jnp.float32)
    conv = conv + jnp.dot(after, taps[2], preferred_element_type=jnp.float32)
    g = jax.nn.gelu(conv + bias, approximate=False).astype(jnp.bfloat16)
    return (x.astype(jnp.float32) + jnp.dot(g, mixing, preferred_element_type=jnp.float32)).astype(
        jnp.bfloat16
    )


def widened_layer(x, gain, taps, bias, mixing, shift):
    count = x.shape[0]
    h = prepare(x, gain)
    return mix(
        x[shift : count - shift],
        h[: count - 2 * shift],
        h[shift : count - shift],
        h[2 * shift :],
        taps,
        bias,
        mixing,
    )


def exchanged_layer(x, gain, taps, bias, mixing, shift):
    chunk = x.shape[0]
    h = prepare(x, gain)
    if shift % chunk == 0:
        before = shifted(h, shift // chunk)
        after = shifted(h, -(shift // chunk))
    else:
        before = jnp.concatenate([shifted(h[chunk - shift :], 1), h[: chunk - shift]], axis=0)
        after = jnp.concatenate([h[shift:], shifted(h[:shift], -1)], axis=0)
    return mix(x, before, h, after, taps, bias, mixing)


def body(sequence_features, norm_gain, conv_weight, conv_bias, mix_weight):
    n_section = lax.axis_size("section")
    my_section = lax.axis_index("section")
    per_section = conv_weight.shape[1]
    block, channels = sequence_features.shape
    first_dilation = block // 2 ** (per_section * n_section - 1)
    group = first_dilation // n_section
    runs = block // first_dilation
    matrices = jnp.concatenate(
        [
            conv_weight.reshape(1, per_section * 3, channels, channels),
            mix_weight.reshape(1, per_section, channels, channels),
        ],
        axis=1,
    )
    vectors = jnp.concatenate([norm_gain, conv_bias], axis=1)
    matrices = lax.all_gather(matrices, "section", tiled=True)
    vectors = lax.all_gather(vectors, "section", tiled=True)
    runs_of = sequence_features.reshape(runs, n_section, group, channels)
    x = lax.dynamic_index_in_dim(runs_of, my_section, axis=1, keepdims=False).reshape(
        runs * group, channels
    )
    chunk = x.shape[0]
    shifts = [first_dilation * 2**index // n_section for index in range(per_section * n_section)]
    widen = sum(shifts[:REDUNDANT])
    assert widen <= chunk
    x = jnp.concatenate([shifted(x[chunk - widen :], 1), x, shifted(x[:widen], -1)], axis=0)
    result = None
    for index, shift in enumerate(shifts):
        step, layer_index = divmod(index, per_section)
        params = (
            vectors[step, layer_index],
            matrices[step, 3 * layer_index : 3 * layer_index + 3],
            vectors[step, per_section + layer_index],
            matrices[step, 3 * per_section + layer_index],
            shift,
        )
        if index < REDUNDANT:
            x = widened_layer(x, *params)
        else:
            x = exchanged_layer(x, *params)
        if layer_index == per_section - 1:
            edge = (x.shape[0] - chunk) // 2
            gathered = lax.all_gather(x[edge : edge + chunk], "section")
            result = gathered if result is None else jnp.where(my_section == step, gathered, result)
    result = result.reshape(n_section, runs, group, channels).transpose(1, 0, 2, 3)
    return result.reshape(1, block, channels)


def solution(mesh):
    in_specs = (
        P("pos", None),
        P("section", None, None),
        P("section", None, None, None, None),
        P("section", None, None),
        P("section", None, None, None),
    )
    out_specs = P("section", "pos", None)
    return jax.shard_map(body, mesh=mesh, in_specs=in_specs, out_specs=out_specs, check_vma=False)
```

profile of v0, /device:TPU:1, one launch (start us, length us, event | category | flops | bytes accessed | tf_op | source)
XLA Modules:
  0.0 166.9 jit_solution(2590244490608321159)
XLA Ops:
  6.5 1.7 %pad_maximum_fusion.1 = bf16[1,8,128,128]{3,2,1,0:T(8,128)(2,1)} fusion(bf16[1,2,128,128]{3,2,1,0:T(8,128)(2,1)} %param.9, bf16[1,6,128,128]{3,2,1,0:T(8,128)(2,1)} %bitcast.185), kind=kLoop, calls=%fused_computation.544 | loop fusion | flops 131072 | bytes 524288 | tf_op jit(solution)/shard_map/concatenate | solution.py:64
  8.3 1.0 dynamic-slice_bitcast_fusion
  9.4 2.5 %collective-permute-start = (bf16[248,128]{1,0:T(8,128)(2,1)S(1)}, bf16[248,128]{1,0:T(8,128)(2,1)S(1)}, u32[]{:S(2)}, u32[]{:S(2)}) collective-permute-start(bf16[248,128]{1,0:T(8,128)(2,1)S(1)} %get-tuple-element.15), channel_id=1, source_target_pairs={{0,4},{4,8},{8,12},{12,16},{16,20},{20,24},{24,28},{28,32},{32,36}... | collective-permute-start | bytes 190472 | tf_op jit(solution)/shard_map/ppermute | solution.py:11
  11.9 8.9 %collective-permute-start.1 = (bf16[248,128]{1,0:T(8,128)(2,1)S(1)}, bf16[248,128]{1,0:T(8,128)(2,1)S(1)}, u32[]{:S(2)}, u32[]{:S(2)}) collective-permute-start(bf16[248,128]{1,0:T(8,128)(2,1)S(1)} %get-tuple-element.16), channel_id=1, source_target_pairs={{0,252},{4,0},{8,4},{12,8},{16,12},{20,16},{24,20},{28,24},{32,28}... | collective-permute-start | bytes 190472 | tf_op jit(solution)/shard_map/ppermute | solution.py:11
  20.8 6.0 %all_gather.30 = f32[4,4,128]{2,1,0:T(4,128)S(1)} all-gather(f32[1,4,128]{2,1,0:T(4,128)S(1)} %pad_maximum_fusion.2), channel_id=1, replica_groups=mesh['pos'=64,'section'=4] {'section'}, dimensions={0}, use_global_device_ids=true | all-gather | bytes 10240 | tf_op jit(solution)/shard_map/all_gather | solution.py:73
  26.8 0.3 fusion.17
  27.1 2.2 %fusion.22 = bf16[1520,128]{1,0:T(8,128)(2,1)S(1)} fusion(bf16[1520,128]{1,0:T(8,128)(2,1)S(1)} %get-tuple-element.6, f32[128]{0:T(128)S(1)} %get-tuple-element.32, f32[1520]{0:T(1024)S(1)} %add_rsqrt_fusion.4), kind=kLoop, calls=%fused_computation.74 | loop fusion | flops 13230080 | bytes 784832 | tf_op jit(solution)/shard_map/convert_element_type | solution.py:17
  29.3 7.3 %all-gather.10.cloned.1.call-done = bf16[4,8,128,128]{3,2,1,0:T(8,128)(2,1)} async-done(((bf16[1,8,128,128]{3,2,1,0:T(8,128)(2,1)}), bf16[4,8,128,128]{3,2,1,0:T(8,128)(2,1)}) %all-gather.10.cloned.1.call-update) | async-done | bytes 1048592 | tf_op jit(solution)/shard_map/all_gather | solution.py:72
  36.6 1.1 fusion.265
  37.8 0.2 convolution_add_fusion.10
  38.1 2.2 %fusion.41 = (f32[1504]{0:T(1024)S(1)}, bf16[1504,128]{1,0:T(8,128)(2,1)S(1)}) fusion(bf16[4,8,128,128]{3,2,1,0:T(8,128)(2,1)S(1)} %copy-done.2, f32[1504,128]{1,0:T(8,128)S(1)} %convolution_add_fusion.10, bf16[1520,128]{1,0:T(8,128)(2,1)S(1)} %fusion.22, f32[128]{0:T(128)S(1)} %get-tuple-element.31, bf16[1520,128]{1,0:T(8,128)(2,1)S(1)} %get-tuple-element.6), kind=kOutput, calls=%fused_computation.93 | convolution fusion | flops 112618016 | bytes 1997184 | tf_op jit(solution)/shard_map/dot_general | solution.py:25
  40.3 2.2 %fusion.46 = bf16[1504,128]{1,0:T(8,128)(2,1)S(1)} fusion(bf16[1504,128]{1,0:T(8,128)(2,1)S(1)} %get-tuple-element.34, f32[128]{0:T(128)S(1)} %get-tuple-element.30, f32[1504]{0:T(1024)S(1)} %add_rsqrt_fusion.3), kind=kLoop, calls=%fused_computation.98 | loop fusion | flops 13090816 | bytes 776576 | tf_op jit(solution)/shard_map/convert_element_type | solution.py:17
  42.5 0.2 fusion.301
  42.7 0.2 convolution_add_fusion.8
  43.0 2.2 %fusion.76 = (f32[1472]{0:T(1024)S(1)}, bf16[1472,128]{1,0:T(8,128)(2,1)S(1)}) fusion(bf16[4,8,128,128]{3,2,1,0:T(8,128)(2,1)S(1)} %copy-done.2, f32[1472,128]{1,0:T(8,128)S(1)} %convolution_add_fusion.8, bf16[1504,128]{1,0:T(8,128)(2,1)S(1)} %fusion.46, f32[128]{0:T(128)S(1)} %get-tuple-element.29, bf16[1504,128]{1,0:T(8,128)(2,1)S(1)} %get-tuple-element.34), kind=kOutput, calls=%fused_computation.137 | convolution fusion | flops 110221888 | bytes 1956096 | tf_op jit(solution)/shard_map/dot_general | solution.py:25
  45.1 0.7 slice.451
  45.9 2.3 %fusion.81 = bf16[1472,128]{1,0:T(8,128)(2,1)S(1)} fusion(bf16[1472,128]{1,0:T(8,128)(2,1)S(1)} %get-tuple-element.36, f32[128]{0:T(128)S(1)} %get-tuple-element.28, f32[1472]{0:T(1024)S(1)} %add_rsqrt_fusion.2), kind=kLoop, calls=%fused_computation.142 | loop fusion | flops 12812288 | bytes 760064 | tf_op jit(solution)/shard_map/convert_element_type | solution.py:17
  48.2 0.2 fusion.337
  48.4 0.2 convolution_add_fusion.5
  48.6 2.0 %fusion.110 = (f32[1408]{0:T(1024)S(1)}, bf16[1408,128]{1,0:T(8,128)(2,1)S(1)}) fusion(bf16[4,8,128,128]{3,2,1,0:T(8,128)(2,1)S(1)} %copy-done.2, f32[1408,128]{1,0:T(8,128)S(1)} %convolution_add_fusion.5, bf16[1472,128]{1,0:T(8,128)(2,1)S(1)} %fusion.81, f32[128]{0:T(128)S(1)} %get-tuple-element.27, bf16[1472,128]{1,0:T(8,128)(2,1)S(1)} %get-tuple-element.36), kind=kOutput, calls=%fused_computation.179 | convolution fusion | flops 105429632 | bytes 1873920 | tf_op jit(solution)/shard_map/dot_general | solution.py:25
  50.7 1.7 %fusion.115 = bf16[1408,128]{1,0:T(8,128)(2,1)S(1)} fusion(bf16[1408,128]{1,0:T(8,128)(2,1)S(1)} %get-tuple-element.38, f32[128]{0:T(128)S(1)} %get-tuple-element.26, f32[1408]{0:T(1024)S(1)} %add_rsqrt_fusion.1), kind=kLoop, calls=%fused_computation.184 | loop fusion | flops 12255232 | bytes 727040 | tf_op jit(solution)/shard_map/convert_element_type | solution.py:17
  52.4 0.2 fusion.373
  52.6 0.2 convolution_add_fusion.2
  52.9 1.9 %fusion.144 = (f32[1280]{0:T(1024)S(1)}, bf16[1280,128]{1,0:T(8,128)(2,1)S(1)}) fusion(bf16[4,8,128,128]{3,2,1,0:T(8,128)(2,1)S(1)} %copy-done.2, f32[1280,128]{1,0:T(8,128)S(1)} %convolution_add_fusion.2, bf16[1408,128]{1,0:T(8,128)(2,1)S(1)} %fusion.115, f32[128]{0:T(128)S(1)} %get-tuple-element.25, bf16[1408,128]{1,0:T(8,128)(2,1)S(1)} %get-tuple-element.38), kind=kOutput, calls=%fused_computation.221 | convolution fusion | flops 95845120 | bytes 1709568 | tf_op jit(solution)/shard_map/dot_general | solution.py:25
  54.8 0.7 slice.417
  55.5 1.5 fusion.149
  57.3 0.2 convolution_add_fusion.22
  57.5 1.6 multiply_reduce_fusion.1
  59.1 1.2 fusion.183
  60.3 1.3 collective-permute-start.2
  61.7 6.4 %collective-permute-start.3 = (bf16[256,128]{1,0:T(8,128)(2,1)S(1)}, bf16[256,128]{1,0:T(8,128)(2,1)S(1)}, u32[]{:S(2)}, u32[]{:S(2)}) collective-permute-start(bf16[256,128]{1,0:T(8,128)(2,1)S(1)} %get-tuple-element.13), channel_id=1, source_target_pairs={{0,252},{4,0},{8,4},{12,8},{16,12},{20,16},{24,20},{28,24},{32,28}... | collective-permute-start | bytes 196616 | tf_op jit(solution)/shard_map/ppermute | solution.py:11
  68.3 1.9 %collective-permute-done.2 = bf16[256,128]{1,0:T(8,128)(2,1)S(1)} collective-permute-done((bf16[256,128]{1,0:T(8,128)(2,1)S(1)}, bf16[256,128]{1,0:T(8,128)(2,1)S(1)}, u32[]{:S(2)}, u32[]{:S(2)}) %collective-permute-start.2) | collective-permute-done | bytes 65568 | tf_op jit(solution)/shard_map/ppermute | solution.py:11
  70.4 1.6 fusion.187
  72.0 1.2 fusion.192
  73.4 7.2 %collective-permute-start.5 = (bf16[512,128]{1,0:T(8,128)(2,1)S(1)}, bf16[512,128]{1,0:T(8,128)(2,1)S(1)}, u32[]{:S(2)}, u32[]{:S(2)}) collective-permute-start(bf16[512,128]{1,0:T(8,128)(2,1)S(1)} %get-tuple-element.10), channel_id=1, source_target_pairs={{0,252},{4,0},{8,4},{12,8},{16,12},{20,16},{24,20},{28,24},{32,28}... | collective-permute-start | bytes 393224 | tf_op jit(solution)/shard_map/ppermute | solution.py:11
  80.7 0.2 fusion.554
  80.9 2.7 %collective-permute-done.4 = bf16[512,128]{1,0:T(8,128)(2,1)S(1)} collective-permute-done((bf16[512,128]{1,0:T(8,128)(2,1)S(1)}, bf16[512,128]{1,0:T(8,128)(2,1)S(1)}, u32[]{:S(2)}, u32[]{:S(2)}) %collective-permute-start.4) | collective-permute-done | bytes 131104 | tf_op jit(solution)/shard_map/ppermute | solution.py:11
  83.6 0.2 convolution_add_fusion.16
  83.9 1.6 multiply_reduce_fusion
  85.4 1.2 fusion.205
  86.8 7.2 %collective-permute-start.7 = (bf16[1024,128]{1,0:T(8,128)(2,1)S(1)}, bf16[1024,128]{1,0:T(8,128)(2,1)S(1)}, u32[]{:S(2)}, u32[]{:S(2)}) collective-permute-start(bf16[1024,128]{1,0:T(8,128)(2,1)S(1)} %fusion.205), channel_id=1, source_target_pairs={{0,252},{4,0},{8,4},{12,8},{16,12},{20,16},{24,20},{28,24},{32,28}... | collective-permute-start | bytes 786440 | tf_op jit(solution)/shard_map/ppermute | solution.py:11
  94.2 4.8 %collective-permute-done.6 = bf16[1024,128]{1,0:T(8,128)(2,1)S(1)} collective-permute-done((bf16[1024,128]{1,0:T(8,128)(2,1)S(1)}, bf16[1024,128]{1,0:T(8,128)(2,1)S(1)}, u32[]{:S(2)}, u32[]{:S(2)}) %collective-permute-start.6) | collective-permute-done | bytes 262176 | tf_op jit(solution)/shard_map/ppermute | solution.py:11
  99.2 2.2 %fusion.16 = bf16[1024,128]{1,0:T(8,128)(2,1)} fusion(f32[1024,128]{1,0:T(8,128)S(1)} %get-tuple-element.46, f32[1024,128]{1,0:T(8,128)S(1)} %convolution_add_fusion.13, bf16[1024,128]{1,0:T(8,128)(2,1)S(1)} %collective-permute-done.7, f32[128]{0:T(128)S(1)} %get-tuple-element.17, bf16[4,8,128,128]{3,2,1,0:T(8,128)(2,1)S(1)} %copy-done.2), kind=kOutput, calls=%fused_computation.39 | convolution fusion | flops 76152832 | bytes 1638912 | tf_op jit(solution)/shard_map/dot_general | solution.py:25
  101.4 4.8 %all-gather.18.cloned.1.call-done = bf16[4096,128]{1,0:T(8,128)(2,1)} async-done(((bf16[1024,128]{1,0:T(8,128)(2,1)}), bf16[4096,128]{1,0:T(8,128)(2,1)}) %all-gather.18.cloned.1.call-update) | async-done | bytes 1048592 | tf_op jit(solution)/shard_map/all_gather | solution.py:99
  106.2 25.7 %all-gather.14.cloned.1.call-done = bf16[4096,128]{1,0:T(8,128)(2,1)} async-done(((bf16[1024,128]{1,0:T(8,128)(2,1)}), bf16[4096,128]{1,0:T(8,128)(2,1)}) %all-gather.14.cloned.1.call-update) | async-done | bytes 1048592 | tf_op jit(solution)/shard_map/all_gather | solution.py:99
  132.0 25.8 %all-gather.12.cloned.1.call-done = bf16[4096,128]{1,0:T(8,128)(2,1)} async-done(((bf16[1024,128]{1,0:T(8,128)(2,1)}), bf16[4096,128]{1,0:T(8,128)(2,1)}) %all-gather.12.cloned.1.call-update) | async-done | bytes 1048592 | tf_op jit(solution)/shard_map/all_gather | solution.py:99
  157.8 1.4 select_select_fusion
  159.2 1.2 copy.13
  (47 shorter events, 1.8 us)
Async XLA Ops:
  6.5 30.1 %all-gather.10.cloned.1.call-start = ((), (), s32[]{:S(2)}) async-start(), calls=%async_computation | async-start | bytes 1310720 | tf_op jit(solution)/shard_map/all_gather | solution.py:72
  8.3 93.2 %all-gather.16.cloned.1.call-start = ((), (), s32[]{:S(2)}) async-start(), calls=%async_computation.3 | async-start | bytes 1310720 | tf_op jit(solution)/shard_map/all_gather | solution.py:99
  9.4 11.4 %copy-start.4 = (f32[1,2,128]{2,1,0:T(2,128)S(1)}, f32[1,2,128]{2,1,0:T(2,128)}, u32[]{:S(2)}) copy-start(f32[1,2,128]{2,1,0:T(2,128)} %param.6) | copy-start | bytes 3076
  9.4 11.4 %copy-start.3 = (f32[1,2,128]{2,1,0:T(2,128)S(1)}, f32[1,2,128]{2,1,0:T(2,128)}, u32[]{:S(2)}) copy-start(f32[1,2,128]{2,1,0:T(2,128)} %param.8) | copy-start | bytes 3076
  9.4 17.4 %collective-permute-start = (bf16[248,128]{1,0:T(8,128)(2,1)S(1)}, bf16[248,128]{1,0:T(8,128)(2,1)S(1)}, u32[]{:S(2)}, u32[]{:S(2)}) collective-permute-start(bf16[248,128]{1,0:T(8,128)(2,1)S(1)} %get-tuple-element.15), channel_id=1, source_target_pairs={{0,4},{4,8},{8,12},{12,16},{16,20},{20,24},{24,28},{28,32},{32,36}... | collective-permute-start | bytes 190472 | tf_op jit(solution)/shard_map/ppermute | solution.py:11
  11.9 14.9 %collective-permute-start.1 = (bf16[248,128]{1,0:T(8,128)(2,1)S(1)}, bf16[248,128]{1,0:T(8,128)(2,1)S(1)}, u32[]{:S(2)}, u32[]{:S(2)}) collective-permute-start(bf16[248,128]{1,0:T(8,128)(2,1)S(1)} %get-tuple-element.16), channel_id=1, source_target_pairs={{0,252},{4,0},{8,4},{12,8},{16,12},{20,16},{24,20},{28,24},{32,28}... | collective-permute-start | bytes 190472 | tf_op jit(solution)/shard_map/ppermute | solution.py:11
  36.6 1.2 copy-start.2
  55.5 50.7 %all-gather.18.cloned.1.call-start = ((), (), s32[]{:S(2)}) async-start(), calls=%async_computation.4 | async-start | bytes 1310720 | tf_op jit(solution)/shard_map/all_gather | solution.py:99
  60.3 9.9 %collective-permute-start.2 = (bf16[256,128]{1,0:T(8,128)(2,1)S(1)}, bf16[256,128]{1,0:T(8,128)(2,1)S(1)}, u32[]{:S(2)}, u32[]{:S(2)}) collective-permute-start(bf16[256,128]{1,0:T(8,128)(2,1)S(1)} %get-tuple-element.14), channel_id=1, source_target_pairs={{0,4},{4,8},{8,12},{12,16},{16,20},{20,24},{24,28},{28,32},{32,36}... | collective-permute-start | bytes 196616 | tf_op jit(solution)/shard_map/ppermute | solution.py:11
  61.7 8.8 %collective-permute-start.3 = (bf16[256,128]{1,0:T(8,128)(2,1)S(1)}, bf16[256,128]{1,0:T(8,128)(2,1)S(1)}, u32[]{:S(2)}, u32[]{:S(2)}) collective-permute-start(bf16[256,128]{1,0:T(8,128)(2,1)S(1)} %get-tuple-element.13), channel_id=1, source_target_pairs={{0,252},{4,0},{8,4},{12,8},{16,12},{20,16},{24,20},{28,24},{32,28}... | collective-permute-start | bytes 196616 | tf_op jit(solution)/shard_map/ppermute | solution.py:11
  68.1 63.9 %all-gather.14.cloned.1.call-start = ((), (), s32[]{:S(2)}) async-start(), calls=%async_computation.2 | async-start | bytes 1310720 | tf_op jit(solution)/shard_map/all_gather | solution.py:99
  72.0 1.3 copy-start
  73.3 10.3 %collective-permute-start.4 = (bf16[512,128]{1,0:T(8,128)(2,1)S(1)}, bf16[512,128]{1,0:T(8,128)(2,1)S(1)}, u32[]{:S(2)}, u32[]{:S(2)}) collective-permute-start(bf16[512,128]{1,0:T(8,128)(2,1)S(1)} %get-tuple-element.9), channel_id=1, source_target_pairs={{0,4},{4,8},{8,12},{12,16},{16,20},{20,24},{24,28},{28,32},{32,36}... | collective-permute-start | bytes 393224 | tf_op jit(solution)/shard_map/ppermute | solution.py:11
  73.4 10.4 %collective-permute-start.5 = (bf16[512,128]{1,0:T(8,128)(2,1)S(1)}, bf16[512,128]{1,0:T(8,128)(2,1)S(1)}, u32[]{:S(2)}, u32[]{:S(2)}) collective-permute-start(bf16[512,128]{1,0:T(8,128)(2,1)S(1)} %get-tuple-element.10), channel_id=1, source_target_pairs={{0,252},{4,0},{8,4},{12,8},{16,12},{20,16},{24,20},{28,24},{32,28}... | collective-permute-start | bytes 393224 | tf_op jit(solution)/shard_map/ppermute | solution.py:11
  80.7 77.1 %all-gather.12.cloned.1.call-start = ((), (), s32[]{:S(2)}) async-start(), calls=%async_computation.1 | async-start | bytes 1310720 | tf_op jit(solution)/shard_map/all_gather | solution.py:99
  80.9 2.9 %copy-start.1 = (bf16[1024,128]{1,0:T(8,128)(2,1)S(1)}, bf16[1024,128]{1,0:T(8,128)(2,1)}, u32[]{:S(2)}) copy-start(bf16[1024,128]{1,0:T(8,128)(2,1)} %copy-done) | copy-start | bytes 786436
  86.7 12.3 %collective-permute-start.6 = (bf16[1024,128]{1,0:T(8,128)(2,1)S(1)}, bf16[1024,128]{1,0:T(8,128)(2,1)S(1)}, u32[]{:S(2)}, u32[]{:S(2)}) collective-permute-start(bf16[1024,128]{1,0:T(8,128)(2,1)S(1)} %fusion.205), channel_id=1, source_target_pairs={{0,4},{4,8},{8,12},{12,16},{16,20},{20,24},{24,28},{28,32},{32,36}... | collective-permute-start | bytes 786440 | tf_op jit(solution)/shard_map/ppermute | solution.py:11
  86.8 12.4 %collective-permute-start.7 = (bf16[1024,128]{1,0:T(8,128)(2,1)S(1)}, bf16[1024,128]{1,0:T(8,128)(2,1)S(1)}, u32[]{:S(2)}, u32[]{:S(2)}) collective-permute-start(bf16[1024,128]{1,0:T(8,128)(2,1)S(1)} %fusion.205), channel_id=1, source_target_pairs={{0,252},{4,0},{8,4},{12,8},{16,12},{20,16},{24,20},{28,24},{32,28}... | collective-permute-start | bytes 786440 | tf_op jit(solution)/shard_map/ppermute | solution.py:11
Sparse Core Ops, SparseCore 0:
  9.1 27.4 all-gather.9
  55.6 26.8 all-gather.15
  84.4 21.8 all-gather.17
  107.9 24.0 all-gather.13
  133.6 24.0 all-gather.11
where the time goes:
time: 167 us
  waiting for transfers between devices  73.1 us (44%)
  starting transfers between devices  33.8 us (20%)
  matrix products  19.5 us (12%)
  other arithmetic  17.1 us (10%)
  between operations  13.5 us (8%)
  blocking collectives  5.98 us (4%)
  local copies, waits for them, and re-layouts  3.88 us (2%)
    all_gather x4, waiting for transfers between devices, body(): gathered = lax.all_gather(x[edge:edge + chunk], 'section')  56.4 us
    ppermute x8, starting transfers between devices, shifted(): lax.ppermute(block, 'pos', [(i, (i + shift) % count) for i in range(count)])  33.6 us
    dot_general x8, matrix products, mix(): jnp.dot(g, mixing, preferred_element_type=jnp.float32)  15.2 us
    convert_element_type x8, other arithmetic, prepare(): jax.nn.gelu(r * lax.rsqrt(meansq + 1e-06) * gain, approximate=False)  13.6 us
    ppermute x8, waiting for transfers between devices, shifted(): lax.ppermute(block, 'pos', [(i, (i + shift) % count) for i in range(count)])  9.34 us
    all_gather x1, waiting for transfers between devices, body(): matrices = lax.all_gather(matrices, 'section', tiled=True)  7.3 us
    all_gather x1, blocking collectives, body(): vectors = lax.all_gather(vectors, 'section', tiled=True)  5.98 us
  transfers between devices with their start and end apart: 13, of which 7 were waited for; matrix products, arithmetic and copies ran while one was open for 10% of the time, Pallas kernels for 0%

commit v1 on v0

--- a/solution.py
+++ b/solution.py
@@ -69,7 +69,9 @@
         axis=1,
     )
     vectors = jnp.concatenate([norm_gain, conv_bias], axis=1)
-    matrices = lax.all_gather(matrices, "section", tiled=True)
+    matrices = jnp.concatenate(
+        lax.all_to_all(jnp.stack([matrices] * lax.axis_size("section")), "section", 0, 0), axis=0
+    )
     vectors = lax.all_gather(vectors, "section", tiled=True)
     runs_of = sequence_features.reshape(runs, n_section, group, channels)
     x = lax.dynamic_index_in_dim(runs_of, my_section, axis=1, keepdims=False).reshape(

time: 167 us -> 169 us (1.012)
  waiting for transfers between devices: 73.1 us -> 62.8 us
  blocking collectives: 5.98 us -> 15.2 us
  starting transfers between devices: 33.8 us -> 38.4 us
  other arithmetic: 17.1 us -> 15.4 us
    all_gather x1, blocking collectives: 5.98 us -> 15.2 us  [body(): vectors = lax.all_gather(vectors, 'section', tiled=True)]
    all_gather x1 -> x0, waiting for transfers between devices: 7.3 us -> none  [body(): matrices = lax.all_gather(matrices, 'section', tiled=True)]
    all_to_all x0 -> x1, starting transfers between devices: none -> 4.57 us  [body(): lax.all_to_all(jnp.stack([matrices] * lax.axis_size('section')), 'section...]
    ppermute x8, waiting for transfers between devices: 9.34 us -> 6.67 us  [shifted(): lax.ppermute(block, 'pos', [(i, (i + shift) % count) for i in range(count)])]
where the time goes in v1:
time: 169 us
  waiting for transfers between devices  62.8 us (37%)
  starting transfers between devices  38.4 us (23%)
  matrix products  18.7 us (11%)
  other arithmetic  15.4 us (9%)
  blocking collectives  15.2 us (9%)
  between operations  13.5 us (8%)
  local copies, waits for them, and re-layouts  4.96 us (3%)
    all_gather x4, waiting for transfers between devices, body(): gathered = lax.all_gather(x[edge:edge + chunk], 'section')  56.1 us
    ppermute x8, starting transfers between devices, shifted(): lax.ppermute(block, 'pos', [(i, (i + shift) % count) for i in range(count)])  33.7 us
    all_gather x1, blocking collectives, body(): vectors = lax.all_gather(vectors, 'section', tiled=True)  15.2 us
    dot_general x8, matrix products, mix(): jnp.dot(g, mixing, preferred_element_type=jnp.float32)  15.2 us
    convert_element_type x8, other arithmetic, prepare(): jax.nn.gelu(r * lax.rsqrt(meansq + 1e-06) * gain, approximate=False)  13.6 us
    ppermute x8, waiting for transfers between devices, shifted(): lax.ppermute(block, 'pos', [(i, (i + shift) % count) for i in range(count)])  6.67 us
    all_to_all x1, starting transfers between devices, body(): lax.all_to_all(jnp.stack([matrices] * lax.axis_size('section')), 'section...  4.57 us
  transfers between devices with their start and end apart: 13, of which 7 were waited for; matrix products, arithmetic and copies ran while one was open for 10% of the time, Pallas kernels for 0%

profile of v1, /device:TPU:1, one launch (start us, length us, event | category | flops | bytes accessed | tf_op | source)
XLA Modules:
  0.0 169.0 jit_solution(7989595870405644881)
XLA Ops:
  6.5 1.0 dynamic-slice_bitcast_fusion
  7.6 2.5 %collective-permute-start = (bf16[248,128]{1,0:T(8,128)(2,1)S(1)}, bf16[248,128]{1,0:T(8,128)(2,1)S(1)}, u32[]{:S(2)}, u32[]{:S(2)}) collective-permute-start(bf16[248,128]{1,0:T(8,128)(2,1)S(1)} %get-tuple-element.15), channel_id=1, source_target_pairs={{0,4},{4,8},{8,12},{12,16},{16,20},{20,24},{24,28},{28,32},{32,36}... | collective-permute-start | bytes 190472 | tf_op jit(solution)/shard_map/ppermute | solution.py:11
  10.2 8.9 %collective-permute-start.1 = (bf16[248,128]{1,0:T(8,128)(2,1)S(1)}, bf16[248,128]{1,0:T(8,128)(2,1)S(1)}, u32[]{:S(2)}, u32[]{:S(2)}) collective-permute-start(bf16[248,128]{1,0:T(8,128)(2,1)S(1)} %get-tuple-element.16), channel_id=1, source_target_pairs={{0,252},{4,0},{8,4},{12,8},{16,12},{20,16},{24,20},{28,24},{32,28}... | collective-permute-start | bytes 190472 | tf_op jit(solution)/shard_map/ppermute | solution.py:11
  19.0 1.2 stack.2
  20.3 4.6 %all-to-all-start = ((bf16[4,1,8,128,128]{4,3,2,1,0:T(8,128)(2,1)}), bf16[4,1,8,128,128]{4,3,2,1,0:T(8,128)(2,1)S(1)}, u32[]{:S(2)}, u32[]{:S(2)}) async-start(bf16[4,1,8,128,128]{4,3,2,1,0:T(8,128)(2,1)} %stack.2), calls=%async_computation | async-start | bytes 2097152 | tf_op jit(solution)/shard_map/all_to_all | solution.py:73
  24.9 15.2 %all_gather.27 = f32[4,4,128]{2,1,0:T(4,128)S(1)} all-gather(f32[1,4,128]{2,1,0:T(4,128)S(1)} %pad_maximum_fusion.1), channel_id=1, replica_groups=mesh['pos'=64,'section'=4] {'section'}, dimensions={0}, use_global_device_ids=true | all-gather | bytes 10240 | tf_op jit(solution)/shard_map/all_gather | solution.py:75
  40.1 0.3 fusion.17
  40.4 2.2 %fusion.22 = bf16[1520,128]{1,0:T(8,128)(2,1)S(1)} fusion(bf16[1520,128]{1,0:T(8,128)(2,1)S(1)} %get-tuple-element.6, f32[128]{0:T(128)S(1)} %get-tuple-element.32, f32[1520]{0:T(1024)S(1)} %add_rsqrt_fusion.4), kind=kLoop, calls=%fused_computation.74 | loop fusion | flops 13230080 | bytes 784832 | tf_op jit(solution)/shard_map/convert_element_type | solution.py:17
  42.6 0.2 fusion.265
  42.9 0.3 convolution_add_fusion.10
  43.1 2.2 %fusion.41 = (f32[1504]{0:T(1024)S(1)}, bf16[1504,128]{1,0:T(8,128)(2,1)S(1)}) fusion(bf16[4,8,128,128]{3,2,1,0:T(8,128)(2,1)S(1)} %bitcast.190, f32[1504,128]{1,0:T(8,128)S(1)} %convolution_add_fusion.10, bf16[1520,128]{1,0:T(8,128)(2,1)S(1)} %fusion.22, f32[128]{0:T(128)S(1)} %get-tuple-element.31, bf16[1520,128]{1,0:T(8,128)(2,1)S(1)} %get-tuple-element.6), kind=kOutput, calls=%fused_computation.93 | convolution fusion | flops 112618016 | bytes 1997184 | tf_op jit(solution)/shard_map/dot_general | solution.py:25
  45.3 2.2 %fusion.46 = bf16[1504,128]{1,0:T(8,128)(2,1)S(1)} fusion(bf16[1504,128]{1,0:T(8,128)(2,1)S(1)} %get-tuple-element.34, f32[128]{0:T(128)S(1)} %get-tuple-element.30, f32[1504]{0:T(1024)S(1)} %add_rsqrt_fusion.3), kind=kLoop, calls=%fused_computation.98 | loop fusion | flops 13090816 | bytes 776576 | tf_op jit(solution)/shard_map/convert_element_type | solution.py:17
  47.5 0.2 fusion.301
  47.8 0.2 convolution_add_fusion.8
  48.0 2.2 %fusion.76 = (f32[1472]{0:T(1024)S(1)}, bf16[1472,128]{1,0:T(8,128)(2,1)S(1)}) fusion(bf16[4,8,128,128]{3,2,1,0:T(8,128)(2,1)S(1)} %bitcast.193, f32[1472,128]{1,0:T(8,128)S(1)} %convolution_add_fusion.8, bf16[1504,128]{1,0:T(8,128)(2,1)S(1)} %fusion.46, f32[128]{0:T(128)S(1)} %get-tuple-element.29, bf16[1504,128]{1,0:T(8,128)(2,1)S(1)} %get-tuple-element.34), kind=kOutput, calls=%fused_computation.137 | convolution fusion | flops 110221888 | bytes 1956096 | tf_op jit(solution)/shard_map/dot_general | solution.py:25
  50.2 2.3 %fusion.81 = bf16[1472,128]{1,0:T(8,128)(2,1)S(1)} fusion(bf16[1472,128]{1,0:T(8,128)(2,1)S(1)} %get-tuple-element.36, f32[128]{0:T(128)S(1)} %get-tuple-element.28, f32[1472]{0:T(1024)S(1)} %add_rsqrt_fusion.2), kind=kLoop, calls=%fused_computation.142 | loop fusion | flops 12812288 | bytes 760064 | tf_op jit(solution)/shard_map/convert_element_type | solution.py:17
  52.5 0.2 fusion.337
  52.8 0.2 convolution_add_fusion.5
  53.0 2.0 %fusion.110 = (f32[1408]{0:T(1024)S(1)}, bf16[1408,128]{1,0:T(8,128)(2,1)S(1)}) fusion(bf16[4,8,128,128]{3,2,1,0:T(8,128)(2,1)S(1)} %bitcast.196, f32[1408,128]{1,0:T(8,128)S(1)} %convolution_add_fusion.5, bf16[1472,128]{1,0:T(8,128)(2,1)S(1)} %fusion.81, f32[128]{0:T(128)S(1)} %get-tuple-element.27, bf16[1472,128]{1,0:T(8,128)(2,1)S(1)} %get-tuple-element.36), kind=kOutput, calls=%fused_computation.179 | convolution fusion | flops 105429632 | bytes 1873920 | tf_op jit(solution)/shard_map/dot_general | solution.py:25
  55.1 1.7 fusion.115
  56.7 0.2 fusion.373
  57.0 0.2 convolution_add_fusion.2
  57.2 1.9 %fusion.144 = (f32[1280]{0:T(1024)S(1)}, bf16[1280,128]{1,0:T(8,128)(2,1)S(1)}) fusion(bf16[4,8,128,128]{3,2,1,0:T(8,128)(2,1)S(1)} %bitcast.199, f32[1280,128]{1,0:T(8,128)S(1)} %convolution_add_fusion.2, bf16[1408,128]{1,0:T(8,128)(2,1)S(1)} %fusion.115, f32[128]{0:T(128)S(1)} %get-tuple-element.25, bf16[1408,128]{1,0:T(8,128)(2,1)S(1)} %get-tuple-element.38), kind=kOutput, calls=%fused_computation.221 | convolution fusion | flops 95845120 | bytes 1709568 | tf_op jit(solution)/shard_map/dot_general | solution.py:25
  59.1 0.7 slice.417
  59.8 1.5 fusion.149
  61.6 0.2 convolution_add_fusion.22
  61.9 1.6 multiply_reduce_fusion.1
  63.5 1.2 fusion.183
  65.0 0.7 slice.451
  65.8 7.2 %collective-permute-start.3 = (bf16[256,128]{1,0:T(8,128)(2,1)S(1)}, bf16[256,128]{1,0:T(8,128)(2,1)S(1)}, u32[]{:S(2)}, u32[]{:S(2)}) collective-permute-start(bf16[256,128]{1,0:T(8,128)(2,1)S(1)} %get-tuple-element.13), channel_id=1, source_target_pairs={{0,252},{4,0},{8,4},{12,8},{16,12},{20,16},{24,20},{28,24},{32,28}... | collective-permute-start | bytes 196616 | tf_op jit(solution)/shard_map/ppermute | solution.py:11
  73.0 1.0 collective-permute-done.2
  74.3 1.6 fusion.187
  75.9 1.2 fusion.192
  77.2 7.7 %collective-permute-start.5 = (bf16[512,128]{1,0:T(8,128)(2,1)S(1)}, bf16[512,128]{1,0:T(8,128)(2,1)S(1)}, u32[]{:S(2)}, u32[]{:S(2)}) collective-permute-start(bf16[512,128]{1,0:T(8,128)(2,1)S(1)} %get-tuple-element.10), channel_id=1, source_target_pairs={{0,252},{4,0},{8,4},{12,8},{16,12},{20,16},{24,20},{28,24},{32,28}... | collective-permute-start | bytes 393224 | tf_op jit(solution)/shard_map/ppermute | solution.py:11
  85.0 0.2 fusion.554
  85.2 2.0 %collective-permute-done.4 = bf16[512,128]{1,0:T(8,128)(2,1)S(1)} collective-permute-done((bf16[512,128]{1,0:T(8,128)(2,1)S(1)}, bf16[512,128]{1,0:T(8,128)(2,1)S(1)}, u32[]{:S(2)}, u32[]{:S(2)}) %collective-permute-start.4) | collective-permute-done | bytes 131104 | tf_op jit(solution)/shard_map/ppermute | solution.py:11
  87.4 1.6 multiply_reduce_fusion
  89.0 1.2 fusion.205
  90.3 7.2 %collective-permute-start.7 = (bf16[1024,128]{1,0:T(8,128)(2,1)S(1)}, bf16[1024,128]{1,0:T(8,128)(2,1)S(1)}, u32[]{:S(2)}, u32[]{:S(2)}) collective-permute-start(bf16[1024,128]{1,0:T(8,128)(2,1)S(1)} %fusion.205), channel_id=1, source_target_pairs={{0,252},{4,0},{8,4},{12,8},{16,12},{20,16},{24,20},{28,24},{32,28}... | collective-permute-start | bytes 786440 | tf_op jit(solution)/shard_map/ppermute | solution.py:11
  97.5 0.2 fusion.553
  97.7 3.6 %collective-permute-done.6 = bf16[1024,128]{1,0:T(8,128)(2,1)S(1)} collective-permute-done((bf16[1024,128]{1,0:T(8,128)(2,1)S(1)}, bf16[1024,128]{1,0:T(8,128)(2,1)S(1)}, u32[]{:S(2)}, u32[]{:S(2)}) %collective-permute-start.6) | collective-permute-done | bytes 262176 | tf_op jit(solution)/shard_map/ppermute | solution.py:11
  101.4 0.2 convolution_add_fusion.13
  101.6 2.2 %fusion.16 = bf16[1024,128]{1,0:T(8,128)(2,1)} fusion(f32[1024,128]{1,0:T(8,128)S(1)} %get-tuple-element.46, f32[1024,128]{1,0:T(8,128)S(1)} %convolution_add_fusion.13, bf16[1024,128]{1,0:T(8,128)(2,1)S(1)} %collective-permute-done.7, f32[128]{0:T(128)S(1)} %get-tuple-element.17, bf16[4,8,128,128]{3,2,1,0:T(8,128)(2,1)S(1)} %bitcast.211), kind=kOutput, calls=%fused_computation.39 | convolution fusion | flops 76152832 | bytes 1638912 | tf_op jit(solution)/shard_map/dot_general | solution.py:25
  103.9 3.1 %all-gather.15.cloned.1.call-done = bf16[4096,128]{1,0:T(8,128)(2,1)} async-done(((bf16[1024,128]{1,0:T(8,128)(2,1)}), bf16[4096,128]{1,0:T(8,128)(2,1)}) %all-gather.15.cloned.1.call-update) | async-done | bytes 1048592 | tf_op jit(solution)/shard_map/all_gather | solution.py:101
  107.0 27.2 %all-gather.11.cloned.1.call-done = bf16[4096,128]{1,0:T(8,128)(2,1)} async-done(((bf16[1024,128]{1,0:T(8,128)(2,1)}), bf16[4096,128]{1,0:T(8,128)(2,1)}) %all-gather.11.cloned.1.call-update) | async-done | bytes 1048592 | tf_op jit(solution)/shard_map/all_gather | solution.py:101
  134.1 25.8 %all-gather.9.cloned.1.call-done = bf16[4096,128]{1,0:T(8,128)(2,1)} async-done(((bf16[1024,128]{1,0:T(8,128)(2,1)}), bf16[4096,128]{1,0:T(8,128)(2,1)}) %all-gather.9.cloned.1.call-update) | async-done | bytes 1048592 | tf_op jit(solution)/shard_map/all_gather | solution.py:101
  159.9 1.4 select_select_fusion
  161.3 1.2 copy.13
  (49 shorter events, 1.5 us)
Async XLA Ops:
  6.5 12.5 %copy-start.3 = (bf16[1,2,128,128]{3,2,1,0:T(8,128)(2,1)S(1)}, bf16[1,2,128,128]{3,2,1,0:T(8,128)(2,1)}, u32[]{:S(2)}) copy-start(bf16[1,2,128,128]{3,2,1,0:T(8,128)(2,1)} %param.9) | copy-start | bytes 196612
  7.6 11.4 %copy-start.2 = (bf16[1,2,3,128,128]{4,3,2,1,0:T(8,128)(2,1)S(1)}, bf16[1,2,3,128,128]{4,3,2,1,0:T(8,128)(2,1)}, u32[]{:S(2)}) copy-start(bf16[1,2,3,128,128]{4,3,2,1,0:T(8,128)(2,1)} %param.7) | copy-start | bytes 589828
  7.6 32.5 %collective-permute-start = (bf16[248,128]{1,0:T(8,128)(2,1)S(1)}, bf16[248,128]{1,0:T(8,128)(2,1)S(1)}, u32[]{:S(2)}, u32[]{:S(2)}) collective-permute-start(bf16[248,128]{1,0:T(8,128)(2,1)S(1)} %get-tuple-element.15), channel_id=1, source_target_pairs={{0,4},{4,8},{8,12},{12,16},{16,20},{20,24},{24,28},{28,32},{32,36}... | collective-permute-start | bytes 190472 | tf_op jit(solution)/shard_map/ppermute | solution.py:11
  10.2 29.9 %collective-permute-start.1 = (bf16[248,128]{1,0:T(8,128)(2,1)S(1)}, bf16[248,128]{1,0:T(8,128)(2,1)S(1)}, u32[]{:S(2)}, u32[]{:S(2)}) collective-permute-start(bf16[248,128]{1,0:T(8,128)(2,1)S(1)} %get-tuple-element.16), channel_id=1, source_target_pairs={{0,252},{4,0},{8,4},{12,8},{16,12},{20,16},{24,20},{28,24},{32,28}... | collective-permute-start | bytes 190472 | tf_op jit(solution)/shard_map/ppermute | solution.py:11
  20.2 4.6 %copy-start.4 = (f32[1,2,128]{2,1,0:T(2,128)S(1)}, f32[1,2,128]{2,1,0:T(2,128)}, u32[]{:S(2)}) copy-start(f32[1,2,128]{2,1,0:T(2,128)} %param.8) | copy-start | bytes 3076
  20.3 4.6 %copy-start.5 = (f32[1,2,128]{2,1,0:T(2,128)S(1)}, f32[1,2,128]{2,1,0:T(2,128)}, u32[]{:S(2)}) copy-start(f32[1,2,128]{2,1,0:T(2,128)} %param.6) | copy-start | bytes 3076
  20.3 22.4 %all-to-all-start = ((bf16[4,1,8,128,128]{4,3,2,1,0:T(8,128)(2,1)}), bf16[4,1,8,128,128]{4,3,2,1,0:T(8,128)(2,1)S(1)}, u32[]{:S(2)}, u32[]{:S(2)}) async-start(bf16[4,1,8,128,128]{4,3,2,1,0:T(8,128)(2,1)} %stack.2), calls=%async_computation | async-start | bytes 2097152 | tf_op jit(solution)/shard_map/all_to_all | solution.py:73
  24.8 79.0 %all-gather.13.cloned.1.call-start = ((), (), s32[]{:S(2)}) async-start(), calls=%async_computation.3 | async-start | bytes 1310720 | tf_op jit(solution)/shard_map/all_gather | solution.py:101
  61.8 45.1 %all-gather.15.cloned.1.call-start = ((), (), s32[]{:S(2)}) async-start(), calls=%async_computation.4 | async-start | bytes 1310720 | tf_op jit(solution)/shard_map/all_gather | solution.py:101
  64.7 9.3 %collective-permute-start.2 = (bf16[256,128]{1,0:T(8,128)(2,1)S(1)}, bf16[256,128]{1,0:T(8,128)(2,1)S(1)}, u32[]{:S(2)}, u32[]{:S(2)}) collective-permute-start(bf16[256,128]{1,0:T(8,128)(2,1)S(1)} %get-tuple-element.14), channel_id=1, source_target_pairs={{0,4},{4,8},{8,12},{12,16},{16,20},{20,24},{24,28},{28,32},{32,36}... | collective-permute-start | bytes 196616 | tf_op jit(solution)/shard_map/ppermute | solution.py:11
  65.8 8.5 %collective-permute-start.3 = (bf16[256,128]{1,0:T(8,128)(2,1)S(1)}, bf16[256,128]{1,0:T(8,128)(2,1)S(1)}, u32[]{:S(2)}, u32[]{:S(2)}) collective-permute-start(bf16[256,128]{1,0:T(8,128)(2,1)S(1)} %get-tuple-element.13), channel_id=1, source_target_pairs={{0,252},{4,0},{8,4},{12,8},{16,12},{20,16},{24,20},{28,24},{32,28}... | collective-permute-start | bytes 196616 | tf_op jit(solution)/shard_map/ppermute | solution.py:11
  73.0 61.1 %all-gather.11.cloned.1.call-start = ((), (), s32[]{:S(2)}) async-start(), calls=%async_computation.2 | async-start | bytes 1310720 | tf_op jit(solution)/shard_map/all_gather | solution.py:101
  75.8 1.3 copy-start
  77.2 10.0 %collective-permute-start.4 = (bf16[512,128]{1,0:T(8,128)(2,1)S(1)}, bf16[512,128]{1,0:T(8,128)(2,1)S(1)}, u32[]{:S(2)}, u32[]{:S(2)}) collective-permute-start(bf16[512,128]{1,0:T(8,128)(2,1)S(1)} %get-tuple-element.9), channel_id=1, source_target_pairs={{0,4},{4,8},{8,12},{12,16},{16,20},{20,24},{24,28},{28,32},{32,36}... | collective-permute-start | bytes 393224 | tf_op jit(solution)/shard_map/ppermute | solution.py:11
  77.2 10.2 %collective-permute-start.5 = (bf16[512,128]{1,0:T(8,128)(2,1)S(1)}, bf16[512,128]{1,0:T(8,128)(2,1)S(1)}, u32[]{:S(2)}, u32[]{:S(2)}) collective-permute-start(bf16[512,128]{1,0:T(8,128)(2,1)S(1)} %get-tuple-element.10), channel_id=1, source_target_pairs={{0,252},{4,0},{8,4},{12,8},{16,12},{20,16},{24,20},{28,24},{32,28}... | collective-permute-start | bytes 393224 | tf_op jit(solution)/shard_map/ppermute | solution.py:11
  84.9 75.0 %all-gather.9.cloned.1.call-start = ((), (), s32[]{:S(2)}) async-start(), calls=%async_computation.1 | async-start | bytes 1310720 | tf_op jit(solution)/shard_map/all_gather | solution.py:101
  85.2 2.2 %copy-start.1 = (bf16[1024,128]{1,0:T(8,128)(2,1)S(1)}, bf16[1024,128]{1,0:T(8,128)(2,1)}, u32[]{:S(2)}) copy-start(bf16[1024,128]{1,0:T(8,128)(2,1)} %copy-done) | copy-start | bytes 786436
  90.2 11.1 %collective-permute-start.6 = (bf16[1024,128]{1,0:T(8,128)(2,1)S(1)}, bf16[1024,128]{1,0:T(8,128)(2,1)S(1)}, u32[]{:S(2)}, u32[]{:S(2)}) collective-permute-start(bf16[1024,128]{1,0:T(8,128)(2,1)S(1)} %fusion.205), channel_id=1, source_target_pairs={{0,4},{4,8},{8,12},{12,16},{16,20},{20,24},{24,28},{28,32},{32,36}... | collective-permute-start | bytes 786440 | tf_op jit(solution)/shard_map/ppermute | solution.py:11
  90.3 11.3 %collective-permute-start.7 = (bf16[1024,128]{1,0:T(8,128)(2,1)S(1)}, bf16[1024,128]{1,0:T(8,128)(2,1)S(1)}, u32[]{:S(2)}, u32[]{:S(2)}) collective-permute-start(bf16[1024,128]{1,0:T(8,128)(2,1)S(1)} %fusion.205), channel_id=1, source_target_pairs={{0,252},{4,0},{8,4},{12,8},{16,12},{20,16},{24,20},{28,24},{32,28}... | collective-permute-start | bytes 786440 | tf_op jit(solution)/shard_map/ppermute | solution.py:11
Sparse Core Ops, SparseCore 0:
  62.0 21.2 all-gather.12
  85.0 21.8 all-gather.14
  108.8 25.2 all-gather.10
  135.8 24.0 all-gather.8
